TPU v7x, 256 devices: a whole 4x4x8 slice. The times are simulated.
256 devices in a mesh: seq: 16 (over x, y), exp: 16 (over z, core).
Axes of the slice: x: 4, y: 4, z: 8, core: 2. Of those that a mesh axis runs over, the one named last changes fastest.
Arguments:
- tokens: bfloat16 [16384, 2048], P('seq', 'exp'), may hold values from -51 to 51
- in_gain: float32 [2048], replicated, may hold values from 0.1 to 1.9
- w_query: bfloat16 [2048, 2048], P(None, 'exp'), may hold values from -0.125 to 0.125
- w_key: bfloat16 [2048, 2048], P(None, 'exp'), may hold values from -0.125 to 0.125
- w_value: bfloat16 [2048, 4096], P(None, 'exp'), may hold values from -0.125 to 0.125
- w_zgate: bfloat16 [2048, 4096], P(None, 'exp'), may hold values from -0.125 to 0.125
- conv_query: float32 [4, 2048], P(None, 'exp'), may hold values from -3 to 3
- conv_key: float32 [4, 2048], P(None, 'exp'), may hold values from -3 to 3
- conv_value: float32 [4, 4096], P(None, 'exp'), may hold values from -3 to 3
- log_decay: float32 [16384, 32], P('seq', 'exp'), may hold values from -1.7 to 0
- write_rate: float32 [16384, 32], P('seq', 'exp'), may hold values from 0 to 1
- norm_gain: float32 [128], replicated, may hold values from 0.1 to 1.9
- w_out: bfloat16 [4096, 2048], P('exp'), may hold values from -0.09375 to 0.09375
- post_gain: float32 [2048], replicated, may hold values from 0.1 to 1.9
- expert_ids: int32 [16384, 2], P(('seq', 'exp')), may hold values from 0 to 15, as said below
- route_weight: float32 [16384, 2], P(('seq', 'exp')), may hold values from 0.1 to 1
- w_gate: bfloat16 [16, 2048, 512], P('exp'), may hold values from -0.125 to 0.125
- w_up: bfloat16 [16, 2048, 512], P('exp'), may hold values from -0.125 to 0.125
- w_down: bfloat16 [16, 512, 2048], P('exp'), may hold values from -0.25 to 0.25
Outputs:
- block_out: bfloat16 [16384, 2048], P(('seq', 'exp'))
Inputs may be any that keep to these rules, and one draw needn't show every extreme that they name: `expert_ids`: each row names 2 different experts. In each aligned block of 64 rows (the rows of one device) no expert is named more than 16 times, and in every aligned block of 1024 rows some expert is named exactly 16 times in each of its blocks of 64 rows.
All inputs are finite; a program needn't handle non-finite values.
Results may differ from a plain program's by a relative error of at most 0.015.
Values may be sent and summed in bfloat16 or wider, within the bound.
No kernel may reach another device: no remote copies, remote signals or barrier semaphores. Data moves between devices by JAX's collectives and lax.ppermute only.
A program may use at most 128 MiB of HBM per device.

v0:
```python
import jax
import jax.numpy as jnp
from jax import lax
from jax.sharding import PartitionSpec as P

DK = 128
DV = 128
STRETCH = 64
EPS = 1e-06
HIGH = lax.Precision.HIGHEST


def passed_along(block, axis, distance):
    devices = range(lax.axis_size(axis))
    route = [(i - distance, i) for i in devices if i - distance in devices]
    return lax.ppermute(block, axis, route)


def rms_scale(values, gain):
    return values * lax.rsqrt(jnp.mean(values * values, -1, keepdims=True) + EPS) * gain


def mix(form, left_arr, right_arr):
    return jnp.einsum(form, left_arr, right_arr, precision=HIGH)


def unit_heads(values, heads):
    shaped = values.reshape(values.shape[0], heads, -1)
    return shaped * lax.rsqrt(jnp.sum(shaped * shaped, -1, keepdims=True) + EPS)


def per_device(
    tokens,
    in_gain,
    w_query,
    w_key,
    w_value,
    w_zgate,
    conv_query,
    conv_key,
    conv_value,
    log_decay,
    write_rate,
    norm_gain,
    w_out,
    post_gain,
    expert_ids,
    route_weight,
    w_gate,
    w_up,
    w_down,
):
    whole = lax.all_gather(tokens, "exp", axis=1, tiled=True)
    x_float = whole.astype(jnp.float32)
    normed = rms_scale(x_float, in_gain).astype(jnp.bfloat16)

    def project(weight):
        return jnp.dot(normed, weight, preferred_element_type=jnp.float32).astype(jnp.bfloat16)

    projected = jnp.concatenate([project(w_query), project(w_key), project(w_value)], 1)
    z_gate = project(w_zgate)
    conv_all = jnp.concatenate([conv_query, conv_key, conv_value], 1)
    taps = conv_all.shape[0]
    length = projected.shape[0]
    tail = projected[length - (taps - 1) :]
    before = passed_along(tail, "seq", 1)
    extended = jnp.concatenate([before, projected], 0).astype(jnp.float32)
    conv_out = conv_all[0] * extended[0:length]
    for index in range(1, taps):
        conv_out = conv_out + conv_all[index] * extended[index : index + length]
    conv_out = jax.nn.silu(conv_out)
    width_q = w_query.shape[1]
    width_k = w_key.shape[1]
    key_heads = width_q // DK
    value_heads = w_value.shape[1] // DV
    group = value_heads // key_heads
    query = unit_heads(conv_out[:, :width_q], key_heads) * DK ** (-0.5)
    keyvec = unit_heads(conv_out[:, width_q : width_q + width_k], key_heads)
    values = conv_out[:, width_q + width_k :].reshape(length, value_heads, DV)
    query = jnp.repeat(query, group, axis=1)
    keyvec = jnp.repeat(keyvec, group, axis=1)
    blocks = length // STRETCH

    def by_block(array):
        return array.reshape(blocks, STRETCH, value_heads, -1).transpose(2, 0, 1, 3)

    q_blk = by_block(query)
    k_blk = by_block(keyvec)
    v_blk = by_block(values)
    g_blk = log_decay.reshape(blocks, STRETCH, value_heads).transpose(2, 0, 1)
    b_blk = write_rate.reshape(blocks, STRETCH, value_heads).transpose(2, 0, 1)
    cumul = jnp.cumsum(g_blk, -1)
    last_cum = cumul[..., -1:]
    places = jnp.arange(STRETCH)
    lower_incl = places[:, None] >= places[None, :]
    lower_strict = places[:, None] > places[None, :]
    spread_log = cumul[..., :, None] - cumul[..., None, :]
    ratio_incl = jnp.where(lower_incl, jnp.exp(jnp.where(lower_incl, spread_log, 0.0)), 0.0)
    key_gram = mix("hnid,hnjd->hnij", k_blk, k_blk)
    system = jnp.eye(STRETCH, dtype=jnp.float32) + jnp.where(
        lower_strict, b_blk[..., None] * key_gram * ratio_incl, 0.0
    )
    decay_in = jnp.exp(cumul)[..., None]
    right_side = jnp.concatenate(
        [b_blk[..., None] * decay_in * k_blk, b_blk[..., None] * v_blk], -1
    )
    solved = jax.scipy.linalg.solve_triangular(system, right_side, lower=True, unit_diagonal=True)
    w_mat = solved[..., :DK]
    u_mat = solved[..., DK:]
    key_tail = k_blk * jnp.exp(last_cum - cumul)[..., None]
    eye_key = jnp.eye(DK, dtype=jnp.float32)
    transit = jnp.exp(last_cum)[..., None] * eye_key - mix("hnik,hnil->hnkl", w_mat, key_tail)
    inject = mix("hniv,hnik->hnvk", u_mat, key_tail)

    def local_step(carry, pair):
        map_pre, add_pre = carry
        map_now, add_now = pair
        new_carry = (
            mix("hkl,hlm->hkm", map_pre, map_now),
            mix("hvl,hlm->hvm", add_pre, map_now) + add_now,
        )
        return (new_carry, carry)

    ident_maps = jnp.broadcast_to(eye_key, (value_heads, DK, DK))
    zero_add = jnp.zeros((value_heads, DV, DK), jnp.float32)
    (map_total, add_total), (map_prefix, add_prefix) = lax.scan(
        local_step,
        (ident_maps, zero_add),
        (transit.transpose(1, 0, 2, 3), inject.transpose(1, 0, 2, 3)),
    )

    def relay(step_index, state):
        passed = mix("hvk,hkl->hvl", state, map_total) + add_total
        return passed_along(passed.astype(jnp.bfloat16), "seq", 1).astype(passed.dtype)

    incoming = lax.fori_loop(0, lax.axis_size("seq") - 1, relay, zero_add)
    starts = (mix("hvk,nhkl->nhvl", incoming, map_prefix) + add_prefix).transpose(1, 0, 2, 3)
    new_values = u_mat - mix("hnik,hnvk->hniv", w_mat, starts)
    scores = mix("hnid,hnjd->hnij", q_blk, k_blk) * ratio_incl
    out_blk = decay_in * mix("hnik,hnvk->hniv", q_blk, starts) + mix(
        "hnij,hnjv->hniv", scores, new_values
    )
    delta_out = out_blk.transpose(1, 2, 0, 3).reshape(length, value_heads, DV)
    gate_z = z_gate.astype(jnp.float32).reshape(length, value_heads, DV)
    gated = (
        (rms_scale(delta_out, norm_gain) * jax.nn.silu(gate_z))
        .astype(jnp.bfloat16)
        .reshape(length, value_heads * DV)
    )
    n_exp = lax.axis_size("exp")
    row_share = length // n_exp
    attn_rows = lax.psum_scatter(
        jnp.dot(gated, w_out, preferred_element_type=jnp.float32).astype(jnp.bfloat16),
        "exp",
        scatter_dimension=0,
        tiled=True,
    ).astype(jnp.float32)
    own_rows = lax.dynamic_slice_in_dim(
        whole, lax.axis_index("exp") * row_share, row_share, 0
    ).astype(jnp.float32)
    resid = own_rows + attn_rows
    post = rms_scale(resid, post_gain).astype(jnp.bfloat16)
    topk = expert_ids.shape[1]
    experts = w_gate.shape[0] * n_exp
    capacity = 2 * row_share * topk // experts
    flat_ids = expert_ids.reshape(-1)
    hits = (flat_ids[:, None] == jnp.arange(experts)[None, :]).astype(jnp.int32)
    earlier_hits = jnp.cumsum(hits, 0) - hits
    slot_of = jnp.sum(earlier_hits * hits, 1)
    target = flat_ids * capacity + slot_of
    route_map = (target[:, None] == jnp.arange(experts * capacity)[None, :]).astype(jnp.bfloat16)
    spread_rows = jnp.repeat(post, topk, axis=0)
    outgoing = jnp.einsum(
        "rp,rd->pd", route_map, spread_rows, preferred_element_type=jnp.float32
    ).astype(jnp.bfloat16)
    outgoing = outgoing.reshape(experts, 1, capacity, post.shape[1])
    batch = lax.all_to_all(outgoing, "exp", split_axis=0, concat_axis=1, tiled=True)
    gate_v = jnp.einsum("esnd,edf->esnf", batch, w_gate, preferred_element_type=jnp.float32)
    up_v = jnp.einsum("esnd,edf->esnf", batch, w_up, preferred_element_type=jnp.float32)
    act = (jax.nn.silu(gate_v) * up_v).astype(jnp.bfloat16)
    processed = jnp.einsum(
        "esnf,efd->esnd", act, w_down, preferred_element_type=jnp.float32
    ).astype(jnp.bfloat16)
    returned = lax.all_to_all(processed, "exp", split_axis=1, concat_axis=0, tiled=True)
    flat_back = returned.reshape(experts * capacity, post.shape[1])
    fetched = jnp.dot(route_map, flat_back, preferred_element_type=jnp.float32).reshape(
        row_share, topk, post.shape[1]
    )
    moe_sum = jnp.sum(route_weight[..., None] * fetched, 1)
    return (resid + moe_sum).astype(jnp.bfloat16)


def solution(mesh):
    return jax.shard_map(
        per_device,
        mesh=mesh,
        in_specs=(
            P("seq", "exp"),
            P(),
            P(None, "exp"),
            P(None, "exp"),
            P(None, "exp"),
            P(None, "exp"),
            P(None, "exp"),
            P(None, "exp"),
            P(None, "exp"),
            P("seq", "exp"),
            P("seq", "exp"),
            P(),
            P("exp", None),
            P(),
            P(("seq", "exp"), None),
            P(("seq", "exp"), None),
            P("exp", None, None),
            P("exp", None, None),
            P("exp", None, None),
        ),
        out_specs=P(("seq", "exp"), None),
        check_vma=False,
    )
```

profile of v0, /device:TPU:1, one launch (start us, length us, event | category | flops | bytes accessed | tf_op | source)
XLA Modules:
  0.0 643.8 jit_solution(5141278856322808113)
XLA Ops:
  15.9 46.7 %all-gather.2.cloned.1.call-done = bf16[1024,2048]{1,0:T(8,128)(2,1)} async-done(((bf16[1024,128]{1,0:T(8,128)(2,1)}), bf16[1024,2048]{1,0:T(8,128)(2,1)}) %all-gather.2.cloned.1.call-update) | async-done | bytes 4194320 | tf_op jit(solution)/shard_map/all_gather | solution.py:53
  62.6 3.2 fusion.16
  68.7 1.5 convolution_convert_fusion.5
  70.2 1.5 convolution_convert_fusion.6
  72.5 3.4 collective-permute-start.1
  76.7 1.5 collective-permute-done.1
  78.2 1.5 maximum_convert_fusion
  79.7 2.2 divide_multiply_fusion
  84.2 3.7 fusion.53
  88.0 158.7 %custom-call.4 = f32[2,16,1,64,64]{3,4,2,1,0:T(8,128)} custom-call(f32[2,16,1,64,64]{4,3,2,1,0:T(8,128)} %fusion.53), custom_call_target="InvertDiagBlocksLowerTriangular" | custom-call | tf_op jit(solution)/shard_map/jit(_solve_triangular)/vmap(vmap())/triangular_solve | solution.py:107
  246.6 1.3 broadcast_multiply_fusion
  248.0 3.3 reshape.217
  251.3 3.3 copy.88
  254.6 1.7 bitcast_multiply_fusion.1
  256.5 2.0 fusion.23
  258.5 5.1 convolution_bitcast_fusion.2
  263.7 5.4 bitcast_subtract_fusion
  269.1 70.9 %while.28 = (s32[]{:T(128)}, f32[2,128,128]{1,2,0:T(8,128)S(1)}, f32[2,128,128]{1,2,0:T(8,128)S(1)}, f32[16,2,128,128]{2,3,0,1:T(8,128)}, f32[16,2,128,128]{2,3,...) while((s32[]{:T(128)}, f32[2,128,128]{1,2,0:T(8,128)S(1)}, ...), condition=%wide.region_5.6_spmd.clone, body=%wide.region_4.5_spmd.clone.sunk | while | flops 100761600 | bytes 2492012 | solution.py:126
  340.2 104.4 %while.29 = (s32[]{:T(128)}, f32[2,128,128]{2,1,0:T(8,128)S(1)}, f32[2,128,128]{2,1,0:T(8,128)S(1)}, f32[2,128,128]{2,1,0:T(8,128)S(1)}, s32[]{:T(128)}, /*index=5*/s32[]{:T(128)}) while((s32[]{:T(128)}, f32[2,128,128]{2,1,0:T(8,128)S(1)}, f32[2,128,128]{2,1,0:T(8,128)S(1)}, f32[2,128,128]{2,1,0:T(8,128)S(1)}, s32[]{:T(128)}, ...), condition=%wide.region_7.8_spmd.clone, body=%wide.region_6.7_spmd.clone.sunk | while | flops 50462720 | bytes 917623 | solution.py:136
  340.6 4.1 collective-permute-start
  344.7 1.3 collective-permute-done
  346.4 3.7 collective-permute-start
  350.1 1.3 collective-permute-done
  351.7 3.7 collective-permute-start
  355.4 1.3 collective-permute-done
  357.0 3.7 collective-permute-start
  360.7 1.3 collective-permute-done
  362.3 5.8 collective-permute-start
  368.1 1.3 collective-permute-done
  369.8 5.8 collective-permute-start
  375.6 1.3 collective-permute-done
  377.2 5.8 collective-permute-start
  383.0 1.3 collective-permute-done
  384.6 5.8 collective-permute-start
  390.4 1.7 collective-permute-done
  392.5 5.7 collective-permute-start
  398.2 1.3 collective-permute-done
  399.8 6.1 collective-permute-start
  405.9 1.3 collective-permute-done
  407.5 6.0 collective-permute-start
  413.5 1.3 collective-permute-done
  415.2 5.8 collective-permute-start
  421.0 1.3 collective-permute-done
  422.6 5.8 collective-permute-start
  428.4 1.3 collective-permute-done
  430.0 5.8 collective-permute-start
  435.8 1.3 collective-permute-done
  437.5 5.8 collective-permute-start
  443.3 1.3 collective-permute-done
  444.6 4.3 bitcast_add_fusion
  449.0 3.1 fusion.44
  453.4 1.8 convolution_multiply_fusion.1
  455.2 2.1 fusion.41
  457.3 1.5 multiply_reduce_fusion
  459.9 1.8 copy.98
  461.8 1.4 mul.305
  463.2 9.4 %convolution_convert_fusion = bf16[1024,2048]{1,0:T(8,128)(2,1)} fusion(bf16[256,2048]{1,0:T(8,128)(2,1)} %param.35, bf16[1024,2048]{1,0:T(8,128)(2,1)} %copy-done.1, bf16[2048,256]{1,0:T(8,128)(2,1)} %param.28, f32[128,8,2,128]{3,2,1,0:T(2,128)S(1)} %bitcast.176, f32[128,8,2,128]{3,2,1,0:T(2,128)} %bitcast.177, f32[256]{0:T(256)S(1)} %copy-done.31), kind=kOutput, calls=%fused_computation.27 | convolution fusion | flops 2152202240 | bytes 12583936 | tf_op jit(solution)/shard_map/dot_general | solution.py:153
  474.1 84.1 %reduce-scatter.2.cloned.1.call-done = bf16[64,2048]{1,0:T(8,128)(2,1)} async-done(((bf16[1024,2048]{1,0:T(8,128)(2,1)}), bf16[64,2048]{1,0:T(8,128)(2,1)}) %reduce-scatter.2.cloned.1.call-update) | async-done | bytes 262160 | tf_op jit(solution)/shard_map/reduce_scatter | solution.py:152
  561.7 36.3 %all_to_all.8 = bf16[16,1,16,2048]{3,2,1,0:T(8,128)(2,1)S(1)} all-to-all(bf16[16,1,16,2048]{3,2,1,0:T(8,128)(2,1)S(1)} %bitcast.174), channel_id=1, replica_groups=mesh['seq'=16,'exp'=16] {'exp'}, dimensions={0} | all-to-all | bytes 2097152 | tf_op jit(solution)/shard_map/all_to_all | solution.py:177
  598.0 1.5 fusion.30
  599.5 4.0 fusion.19
  603.5 3.7 all-to-all-start.1
  607.4 27.1 %all-to-all-done.1 = bf16[1,16,16,2048]{3,2,0,1:T(8,128)(2,1)S(1)} async-done(((bf16[1,16,16,2048]{3,2,0,1:T(8,128)(2,1)}), bf16[1,16,16,2048]{3,2,0,1:T(8,128)(2,1)S(1)}, u32[]{:S(2)}, u32[]{:S(2)}) %all-to-all-start.1) | async-done | bytes 1048608 | tf_op jit(solution)/shard_map/all_to_all | solution.py:184
  635.0 1.7 add_convert_fusion
  (261 shorter events, 98.2 us)
Async XLA Ops:
  6.5 593.0 %copy-start = (bf16[1,512,2048]{2,1,0:T(8,128)(2,1)S(1)}, bf16[1,512,2048]{2,1,0:T(8,128)(2,1)}, u32[]{:S(2)}) copy-start(bf16[1,512,2048]{2,1,0:T(8,128)(2,1)} %param.41) | copy-start | bytes 6291460
  6.5 56.1 %all-gather.2.cloned.1.call-start = ((), (), s32[]{:S(2)}) async-start(), calls=%async_computation.3 | async-start | bytes 4456448 | tf_op jit(solution)/shard_map/all_gather | solution.py:53
  7.3 550.9 %reduce-scatter.2.cloned.1.call-start = ((), (), s32[]{:S(2)}) async-start(), calls=%async_computation.4 | async-start | bytes 4456448 | tf_op jit(solution)/shard_map/reduce_scatter | solution.py:152
  8.9 57.0 %copy-start.15 = (f32[16,64,2]{1,0,2:T(8,128)}, f32[16,64,2]{1,0,2:T(8,128)S(1)}, u32[]{:S(2)}) copy-start(f32[16,64,2]{1,0,2:T(8,128)S(1)} %reshape.203) | copy-start | bytes 24580
  15.9 49.9 %copy-start.20 = (f32[2048]{0:T(1024)S(1)}, f32[2048]{0:T(1024)}, u32[]{:S(2)}) copy-start(f32[2048]{0:T(1024)} %param.24) | copy-start | bytes 24580
  62.6 3.4 copy-start.2
  66.1 1.2 copy-start.30
  67.3 2.9 copy-start.1
  67.3 1.4 copy-start.12
  68.7 1.5 copy-start.13
  72.5 5.7 collective-permute-start.1
  76.7 3.0 copy-start.22
  76.7 3.0 copy-start.23
  76.7 3.0 copy-start.24
  76.7 3.0 copy-start.25
  84.2 162.4 %copy-start.18 = (f32[2,16,64]{2,1,0:T(8,128)S(1)}, f32[2,16,64]{2,1,0:T(8,128)}, u32[]{:S(2)}) copy-start(f32[2,16,64]{2,1,0:T(8,128)} %get-tuple-element.187) | copy-start | bytes 24580
  251.3 3.3 copy-start.16
  254.6 1.7 copy-start.7
  254.6 1.9 copy-start.11
  256.5 2.1 copy-start.14
  258.5 10.6 %copy-start.5 = (f32[2,16,64,256]{3,2,1,0:T(8,128)}, f32[2,16,64,256]{3,2,1,0:T(8,128)S(1)}, u32[]{:S(2)}) copy-start(f32[2,16,64,256]{3,2,1,0:T(8,128)S(1)} %fusion.23) | copy-start | bytes 6291460
  258.5 5.2 copy-start.27
  340.6 5.4 collective-permute-start
  346.4 5.0 collective-permute-start
  351.7 5.0 collective-permute-start
  357.0 5.0 collective-permute-start
  362.3 7.1 %collective-permute-start = (bf16[2,128,128]{2,1,0:T(8,128)(2,1)S(1)}, bf16[2,128,128]{2,1,0:T(8,128)(2,1)S(1)}, u32[]{:S(2)}, u32[]{:S(2)}) collective-permute-start(bf16[2,128,128]{2,1,0:T(8,128)(2,1)S(1)} %fusion.141), channel_id=1, source_target_pairs={{0,16},{16,32},{32,48},{48,64},{64,80},{80,96},{96,112},{112,128},... | collective-permute-start | bytes 196616 | tf_op jit(solution)/shard_map/while/body/eval_jaxpr/ppermute | solution.py:16
  369.8 7.1 %collective-permute-start = (bf16[2,128,128]{2,1,0:T(8,128)(2,1)S(1)}, bf16[2,128,128]{2,1,0:T(8,128)(2,1)S(1)}, u32[]{:S(2)}, u32[]{:S(2)}) collective-permute-start(bf16[2,128,128]{2,1,0:T(8,128)(2,1)S(1)} %fusion.141), channel_id=1, source_target_pairs={{0,16},{16,32},{32,48},{48,64},{64,80},{80,96},{96,112},{112,128},... | collective-permute-start | bytes 196616 | tf_op jit(solution)/shard_map/while/body/eval_jaxpr/ppermute | solution.py:16
  377.2 7.1 %collective-permute-start = (bf16[2,128,128]{2,1,0:T(8,128)(2,1)S(1)}, bf16[2,128,128]{2,1,0:T(8,128)(2,1)S(1)}, u32[]{:S(2)}, u32[]{:S(2)}) collective-permute-start(bf16[2,128,128]{2,1,0:T(8,128)(2,1)S(1)} %fusion.141), channel_id=1, source_target_pairs={{0,16},{16,32},{32,48},{48,64},{64,80},{80,96},{96,112},{112,128},... | collective-permute-start | bytes 196616 | tf_op jit(solution)/shard_map/while/body/eval_jaxpr/ppermute | solution.py:16
  384.6 7.5 %collective-permute-start = (bf16[2,128,128]{2,1,0:T(8,128)(2,1)S(1)}, bf16[2,128,128]{2,1,0:T(8,128)(2,1)S(1)}, u32[]{:S(2)}, u32[]{:S(2)}) collective-permute-start(bf16[2,128,128]{2,1,0:T(8,128)(2,1)S(1)} %fusion.141), channel_id=1, source_target_pairs={{0,16},{16,32},{32,48},{48,64},{64,80},{80,96},{96,112},{112,128},... | collective-permute-start | bytes 196616 | tf_op jit(solution)/shard_map/while/body/eval_jaxpr/ppermute | solution.py:16
  392.5 7.0 %collective-permute-start = (bf16[2,128,128]{2,1,0:T(8,128)(2,1)S(1)}, bf16[2,128,128]{2,1,0:T(8,128)(2,1)S(1)}, u32[]{:S(2)}, u32[]{:S(2)}) collective-permute-start(bf16[2,128,128]{2,1,0:T(8,128)(2,1)S(1)} %fusion.141), channel_id=1, source_target_pairs={{0,16},{16,32},{32,48},{48,64},{64,80},{80,96},{96,112},{112,128},... | collective-permute-start | bytes 196616 | tf_op jit(solution)/shard_map/while/body/eval_jaxpr/ppermute | solution.py:16
  399.8 7.4 %collective-permute-start = (bf16[2,128,128]{2,1,0:T(8,128)(2,1)S(1)}, bf16[2,128,128]{2,1,0:T(8,128)(2,1)S(1)}, u32[]{:S(2)}, u32[]{:S(2)}) collective-permute-start(bf16[2,128,128]{2,1,0:T(8,128)(2,1)S(1)} %fusion.141), channel_id=1, source_target_pairs={{0,16},{16,32},{32,48},{48,64},{64,80},{80,96},{96,112},{112,128},... | collective-permute-start | bytes 196616 | tf_op jit(solution)/shard_map/while/body/eval_jaxpr/ppermute | solution.py:16
  407.5 7.4 %collective-permute-start = (bf16[2,128,128]{2,1,0:T(8,128)(2,1)S(1)}, bf16[2,128,128]{2,1,0:T(8,128)(2,1)S(1)}, u32[]{:S(2)}, u32[]{:S(2)}) collective-permute-start(bf16[2,128,128]{2,1,0:T(8,128)(2,1)S(1)} %fusion.141), channel_id=1, source_target_pairs={{0,16},{16,32},{32,48},{48,64},{64,80},{80,96},{96,112},{112,128},... | collective-permute-start | bytes 196616 | tf_op jit(solution)/shard_map/while/body/eval_jaxpr/ppermute | solution.py:16
  415.2 7.1 %collective-permute-start = (bf16[2,128,128]{2,1,0:T(8,128)(2,1)S(1)}, bf16[2,128,128]{2,1,0:T(8,128)(2,1)S(1)}, u32[]{:S(2)}, u32[]{:S(2)}) collective-permute-start(bf16[2,128,128]{2,1,0:T(8,128)(2,1)S(1)} %fusion.141), channel_id=1, source_target_pairs={{0,16},{16,32},{32,48},{48,64},{64,80},{80,96},{96,112},{112,128},... | collective-permute-start | bytes 196616 | tf_op jit(solution)/shard_map/while/body/eval_jaxpr/ppermute | solution.py:16
  422.6 7.1 %collective-permute-start = (bf16[2,128,128]{2,1,0:T(8,128)(2,1)S(1)}, bf16[2,128,128]{2,1,0:T(8,128)(2,1)S(1)}, u32[]{:S(2)}, u32[]{:S(2)}) collective-permute-start(bf16[2,128,128]{2,1,0:T(8,128)(2,1)S(1)} %fusion.141), channel_id=1, source_target_pairs={{0,16},{16,32},{32,48},{48,64},{64,80},{80,96},{96,112},{112,128},... | collective-permute-start | bytes 196616 | tf_op jit(solution)/shard_map/while/body/eval_jaxpr/ppermute | solution.py:16
  430.0 7.1 %collective-permute-start = (bf16[2,128,128]{2,1,0:T(8,128)(2,1)S(1)}, bf16[2,128,128]{2,1,0:T(8,128)(2,1)S(1)}, u32[]{:S(2)}, u32[]{:S(2)}) collective-permute-start(bf16[2,128,128]{2,1,0:T(8,128)(2,1)S(1)} %fusion.141), channel_id=1, source_target_pairs={{0,16},{16,32},{32,48},{48,64},{64,80},{80,96},{96,112},{112,128},... | collective-permute-start | bytes 196616 | tf_op jit(solution)/shard_map/while/body/eval_jaxpr/ppermute | solution.py:16
  437.5 7.1 %collective-permute-start = (bf16[2,128,128]{2,1,0:T(8,128)(2,1)S(1)}, bf16[2,128,128]{2,1,0:T(8,128)(2,1)S(1)}, u32[]{:S(2)}, u32[]{:S(2)}) collective-permute-start(bf16[2,128,128]{2,1,0:T(8,128)(2,1)S(1)} %fusion.141), channel_id=1, source_target_pairs={{0,16},{16,32},{32,48},{48,64},{64,80},{80,96},{96,112},{112,128},... | collective-permute-start | bytes 196616 | tf_op jit(solution)/shard_map/while/body/eval_jaxpr/ppermute | solution.py:16
  444.6 4.4 copy-start.6
  449.0 3.1 copy-start.3
  449.0 4.4 copy-start.19
  452.1 3.1 copy-start.17
  453.4 1.9 copy-start.4
  455.2 2.1 copy-start.8
  458.8 4.4 copy-start.31
  459.9 1.9 copy-start.10
  472.7 0.7 copy-start.26
  472.7 86.7 %copy-start.21 = (f32[2048]{0:T(1024)S(1)}, f32[2048]{0:T(1024)}, u32[]{:S(2)}) copy-start(f32[2048]{0:T(1024)} %param.36) | copy-start | bytes 24580
  561.1 36.9 %copy-start.29 = (bf16[1,2048,512]{2,1,0:T(8,128)(2,1)S(1)}, bf16[1,2048,512]{2,1,0:T(8,128)(2,1)}, u32[]{:S(2)}) copy-start(bf16[1,2048,512]{2,1,0:T(8,128)(2,1)} %param.39) | copy-start | bytes 6291460
  603.5 31.1 %copy-start.28 = (f32[64,2]{0,1:T(2,128)S(1)}, f32[64,2]{0,1:T(2,128)}, u32[]{:S(2)}) copy-start(f32[64,2]{0,1:T(2,128)} %param.38) | copy-start | bytes 1540
  603.5 31.4 %copy-start.9 = (bf16[64,2048]{1,0:T(8,128)(2,1)S(1)}, bf16[64,2048]{1,0:T(8,128)(2,1)}, u32[]{:S(2)}) copy-start(bf16[64,2048]{1,0:T(8,128)(2,1)} %reduce-scatter.2.cloned.1.call-done) | copy-start | bytes 786436
  603.5 31.0 %all-to-all-start.1 = ((bf16[1,16,16,2048]{3,2,0,1:T(8,128)(2,1)}), bf16[1,16,16,2048]{3,2,0,1:T(8,128)(2,1)S(1)}, u32[]{:S(2)}, u32[]{:S(2)}) async-start(bf16[1,16,16,2048]{3,2,0,1:T(8,128)(2,1)} %fusion.19), calls=%async_computation.2 | async-start | bytes 2097152 | tf_op jit(solution)/shard_map/all_to_all | solution.py:184
Sparse Core Ops, SparseCore 0:
  9.1 53.4 all-gather.1
  472.8 85.3 reduce-scatter.1
where the time goes:
time: 653 us; the launch traced here: 644 us
  other arithmetic  191 us (29%)
  waiting for transfers between devices  180 us (28%)
  matrix products  95 us (15%)
  starting transfers between devices  86.6 us (13%)
  local copies, waits for them, and re-layouts  38.7 us (6%)
  blocking collectives  36.3 us (6%)
  between operations  14.2 us (2%)
    another operation x4, other arithmetic, per_device(): jax.scipy.linalg.solve_triangular(system, right_side, lower=True, unit_di...  160 us
    reduce_scatter x1, waiting for transfers between devices, per_device(): lax.psum_scatter(jnp.dot(gated, w_out, preferred_element_type=jnp.float32...  84.1 us
    ppermute x16, starting transfers between devices, passed_along(): return lax.ppermute(block, axis, route)  82.8 us
    dot_general x55, matrix products, mix(): return jnp.einsum(form, left_arr, right_arr, precision=HIGH)  72.8 us
    all_gather x1, waiting for transfers between devices, per_device(): whole = lax.all_gather(tokens, 'exp', axis=1, tiled=True)  46.7 us
    all_to_all x1, blocking collectives, per_device(): lax.all_to_all(outgoing, 'exp', split_axis=0, concat_axis=1, tiled=True)  36.3 us
    all_to_all x1, waiting for transfers between devices, per_device(): lax.all_to_all(processed, 'exp', split_axis=1, concat_axis=0, tiled=True)  27.1 us
    ppermute x16, waiting for transfers between devices, passed_along(): return lax.ppermute(block, axis, route)  21.6 us
  transfers between devices with their start and end apart: 19, of which 19 were waited for; matrix products, arithmetic and copies ran while one was open for 2% of the time, Pallas kernels for 0%

commit v1 on v0

--- a/solution.py
+++ b/solution.py
@@ -50,7 +50,9 @@
     w_up,
     w_down,
 ):
-    whole = lax.all_gather(tokens, "exp", axis=1, tiled=True)
+    whole = jnp.concatenate(
+        lax.all_to_all(jnp.stack([tokens] * lax.axis_size("exp")), "exp", 0, 0), axis=1
+    )
     x_float = whole.astype(jnp.float32)
     normed = rms_scale(x_float, in_gain).astype(jnp.bfloat16)
 

time: 653 us -> 712 us (1.090)
  waiting for transfers between devices: 180 us -> 218 us
  starting transfers between devices: 86.6 us -> 96.4 us
    all_to_all x0 -> x1, waiting for transfers between devices: none -> 88.9 us  [per_device(): lax.all_to_all(jnp.stack([tokens] * lax.axis_size('exp')), 'exp', 0, 0)]
    all_gather x1 -> x0, waiting for transfers between devices: 46.7 us -> none  [per_device(): whole = lax.all_gather(tokens, 'exp', axis=1, tiled=True)]
    all_to_all x0 -> x1, starting transfers between devices: none -> 10.1 us  [per_device(): lax.all_to_all(jnp.stack([tokens] * lax.axis_size('exp')), 'exp', 0, 0)]
where the time goes in v1:
time: 712 us; the launch traced here: 702 us
  waiting for transfers between devices  218 us (31%)
  other arithmetic  190 us (27%)
  matrix products  102 us (14%)
  starting transfers between devices  96.4 us (14%)
  local copies, waits for them, and re-layouts  42.8 us (6%)
  blocking collectives  36.5 us (5%)
  between operations  14.3 us (2%)
    another operation x4, other arithmetic, per_device(): jax.scipy.linalg.solve_triangular(system, right_side, lower=True, unit_di...  160 us
    all_to_all x1, waiting for transfers between devices, per_device(): lax.all_to_all(jnp.stack([tokens] * lax.axis_size('exp')), 'exp', 0, 0)  88.9 us
    ppermute x16, starting transfers between devices, passed_along(): return lax.ppermute(block, axis, route)  82.5 us
    reduce_scatter x1, waiting for transfers between devices, per_device(): lax.psum_scatter(jnp.dot(gated, w_out, preferred_element_type=jnp.float32...  81.1 us
    dot_general x55, matrix products, mix(): return jnp.einsum(form, left_arr, right_arr, precision=HIGH)  72.8 us
    all_to_all x1, blocking collectives, per_device(): lax.all_to_all(outgoing, 'exp', split_axis=0, concat_axis=1, tiled=True)  36.5 us
    all_to_all x1, waiting for transfers between devices, per_device(): lax.all_to_all(processed, 'exp', split_axis=1, concat_axis=0, tiled=True)  27.1 us
    ppermute x16, waiting for transfers between devices, passed_along(): return lax.ppermute(block, axis, route)  21.2 us
  transfers between devices with their start and end apart: 19, of which 19 were waited for; matrix products, arithmetic and copies ran while one was open for 2% of the time, Pallas kernels for 0%

profile of v1, /device:TPU:1, one launch (start us, length us, event | category | flops | bytes accessed | tf_op | source)
XLA Modules:
  0.0 702.1 jit_solution(474170628864919647)
XLA Ops:
  6.5 3.9 stack.2
  10.5 10.1 %all-to-all-start = ((bf16[16,1024,128]{2,1,0:T(8,128)(2,1)}), bf16[16,1024,128]{2,1,0:T(8,128)(2,1)}, u32[]{:S(2)}, u32[]{:S(2)}) async-start(bf16[16,1024,128]{2,1,0:T(8,128)(2,1)} %stack.2), calls=%async_computation | async-start | bytes 8388608 | tf_op jit(solution)/shard_map/all_to_all | solution.py:54
  25.2 88.9 %all-to-all-done = bf16[16,1024,128]{2,1,0:T(8,128)(2,1)} async-done(((bf16[16,1024,128]{2,1,0:T(8,128)(2,1)}), bf16[16,1024,128]{2,1,0:T(8,128)(2,1)}, u32[]{:S(2)}, u32[]{:S(2)}) %all-to-all-start) | async-done | bytes 4194336 | tf_op jit(solution)/shard_map/all_to_all | solution.py:54
  114.1 3.2 multiply_reduce_fusion
  117.3 3.8 convolution_convert_fusion.4
  121.1 3.8 convolution_convert_fusion.5
  124.9 3.7 convolution_convert_fusion.6
  129.4 3.9 collective-permute-start.1
  134.9 1.5 maximum_convert_fusion
  136.4 2.2 divide_multiply_fusion
  140.9 3.7 fusion.50
  144.6 158.7 %custom-call.4 = f32[2,16,1,64,64]{3,4,2,1,0:T(8,128)} custom-call(f32[2,16,1,64,64]{4,3,2,1,0:T(8,128)} %fusion.50), custom_call_target="InvertDiagBlocksLowerTriangular" | custom-call | tf_op jit(solution)/shard_map/jit(_solve_triangular)/vmap(vmap())/triangular_solve | solution.py:109
  303.3 1.4 broadcast_multiply_fusion
  304.7 3.3 reshape.227
  308.0 3.3 copy.90
  311.3 1.7 bitcast_multiply_fusion.1
  313.1 2.0 fusion.20
  315.2 5.2 convolution_bitcast_fusion.2
  320.4 5.4 bitcast_subtract_fusion
  325.8 70.9 %while.28 = (s32[]{:T(128)}, f32[2,128,128]{1,2,0:T(8,128)S(1)}, f32[2,128,128]{1,2,0:T(8,128)S(1)}, f32[16,2,128,128]{2,3,0,1:T(8,128)}, f32[16,2,128,128]{2,3,...) while((s32[]{:T(128)}, f32[2,128,128]{1,2,0:T(8,128)S(1)}, ...), condition=%wide.region_5.6_spmd.clone, body=%wide.region_4.5_spmd.clone.sunk | while | flops 100761600 | bytes 2492012 | solution.py:128
  397.0 104.0 %while.29 = (s32[]{:T(128)}, f32[2,128,128]{2,1,0:T(8,128)S(1)}, f32[2,128,128]{2,1,0:T(8,128)S(1)}, f32[2,128,128]{2,1,0:T(8,128)S(1)}, s32[]{:T(128)}, /*index=5*/s32[]{:T(128)}) while((s32[]{:T(128)}, f32[2,128,128]{2,1,0:T(8,128)S(1)}, f32[2,128,128]{2,1,0:T(8,128)S(1)}, f32[2,128,128]{2,1,0:T(8,128)S(1)}, s32[]{:T(128)}, ...), condition=%wide.region_7.8_spmd.clone, body=%wide.region_6.7_spmd.clone.sunk | while | flops 50462720 | bytes 917623 | solution.py:138
  397.4 3.8 collective-permute-start
  401.2 1.3 collective-permute-done
  402.8 3.7 collective-permute-start
  406.5 1.3 collective-permute-done
  408.1 3.7 collective-permute-start
  411.9 1.3 collective-permute-done
  413.5 3.7 collective-permute-start
  417.2 1.5 collective-permute-done
  418.9 5.6 collective-permute-start
  424.5 1.3 collective-permute-done
  426.2 5.8 collective-permute-start
  432.0 1.3 collective-permute-done
  433.6 5.8 collective-permute-start
  439.4 1.9 collective-permute-done
  441.6 5.5 collective-permute-start
  447.1 1.3 collective-permute-done
  448.8 5.8 collective-permute-start
  454.6 1.3 collective-permute-done
  456.2 6.0 collective-permute-start
  463.8 5.8 collective-permute-start
  471.2 5.8 collective-permute-start
  477.0 1.3 collective-permute-done
  478.6 5.8 collective-permute-start
  486.1 5.8 collective-permute-start
  491.9 1.3 collective-permute-done
  493.5 6.1 collective-permute-start
  499.6 1.3 collective-permute-done
  501.0 4.3 bitcast_add_fusion
  505.4 3.1 fusion.41
  509.7 1.8 convolution_multiply_fusion.1
  511.6 2.1 fusion.38
  513.7 1.5 multiply_reduce_fusion.1
  516.3 1.8 copy.100
  518.1 1.4 mul.306
  519.6 9.5 %convolution_convert_fusion = bf16[1024,2048]{1,0:T(8,128)(2,1)} fusion(bf16[256,2048]{1,0:T(8,128)(2,1)} %param.35, bf16[2048,256]{1,0:T(8,128)(2,1)} %param.28, f32[128,8,2,128]{3,2,1,0:T(2,128)S(1)} %bitcast.199, f32[128,8,2,128]{3,2,1,0:T(2,128)} %bitcast.200, f32[256]{0:T(256)S(1)} %copy-done.38, f32[2048]{0:T(1024)S(1)} %copy-done.36, ...), kind=kOutput, calls=%fused_computation.25 | convolution fusion | flops 2160590848 | bytes 12596224 | tf_op jit(solution)/shard_map/dot_general | solution.py:155
  530.5 4.8 copy_bitcast_fusion
  535.3 81.1 %reduce-scatter.2.cloned.1.call-done = bf16[64,2048]{1,0:T(8,128)(2,1)} async-done(((bf16[1024,2048]{1,0:T(8,128)(2,1)}), bf16[64,2048]{1,0:T(8,128)(2,1)}) %reduce-scatter.2.cloned.1.call-update) | async-done | bytes 262160 | tf_op jit(solution)/shard_map/reduce_scatter | solution.py:154
  619.9 36.5 %all_to_all.23 = bf16[16,1,16,2048]{3,2,1,0:T(8,128)(2,1)S(1)} all-to-all(bf16[16,1,16,2048]{3,2,1,0:T(8,128)(2,1)S(1)} %bitcast.197), channel_id=1, replica_groups=mesh['seq'=16,'exp'=16] {'exp'}, dimensions={0} | all-to-all | bytes 2097152 | tf_op jit(solution)/shard_map/all_to_all | solution.py:179
  656.3 1.5 fusion.27
  657.8 4.0 fusion.16
  661.9 3.7 all-to-all-start.2
  665.8 27.1 %all-to-all-done.2 = bf16[1,16,16,2048]{3,2,0,1:T(8,128)(2,1)S(1)} async-done(((bf16[1,16,16,2048]{3,2,0,1:T(8,128)(2,1)}), bf16[1,16,16,2048]{3,2,0,1:T(8,128)(2,1)S(1)}, u32[]{:S(2)}, u32[]{:S(2)}) %all-to-all-start.2) | async-done | bytes 1048608 | tf_op jit(solution)/shard_map/all_to_all | solution.py:186
  693.3 1.7 add_convert_fusion
  (275 shorter events, 95.4 us)
Async XLA Ops:
  6.5 651.3 %copy-start = (bf16[1,512,2048]{2,1,0:T(8,128)(2,1)S(1)}, bf16[1,512,2048]{2,1,0:T(8,128)(2,1)}, u32[]{:S(2)}) copy-start(bf16[1,512,2048]{2,1,0:T(8,128)(2,1)} %param.41) | copy-start | bytes 6291460
  10.4 10.2 %copy-start.21 = (f32[1024,2]{0,1:T(2,128)S(1)}, f32[1024,2]{0,1:T(2,128)}, u32[]{:S(2)}) copy-start(f32[1024,2]{0,1:T(2,128)} %param.32) | copy-start | bytes 24580
  10.4 10.3 %copy-start.22 = (f32[1024,2]{0,1:T(2,128)S(1)}, f32[1024,2]{0,1:T(2,128)}, u32[]{:S(2)}) copy-start(f32[1024,2]{0,1:T(2,128)} %param.33) | copy-start | bytes 24580
  10.4 10.8 %copy-start.28 = (f32[4,128]{1,0:T(4,128)S(1)}, f32[4,128]{1,0:T(4,128)}, u32[]{:S(2)}) copy-start(f32[4,128]{1,0:T(4,128)} %param.29) | copy-start | bytes 6148
  10.4 10.8 %copy-start.29 = (f32[4,128]{1,0:T(4,128)S(1)}, f32[4,128]{1,0:T(4,128)}, u32[]{:S(2)}) copy-start(f32[4,128]{1,0:T(4,128)} %param.30) | copy-start | bytes 6148
  10.5 10.8 %copy-start.24 = (f32[4,256]{1,0:T(4,128)S(1)}, f32[4,256]{1,0:T(4,128)}, u32[]{:S(2)}) copy-start(f32[4,256]{1,0:T(4,128)} %param.31) | copy-start | bytes 12292
  10.5 12.2 %copy-start.37 = (f32[128]{0:T(128)S(1)}, f32[128]{0:T(128)}, u32[]{:S(2)}) copy-start(f32[128]{0:T(128)} %param.34) | copy-start | bytes 1540
  10.5 103.6 %all-to-all-start = ((bf16[16,1024,128]{2,1,0:T(8,128)(2,1)}), bf16[16,1024,128]{2,1,0:T(8,128)(2,1)}, u32[]{:S(2)}, u32[]{:S(2)}) async-start(bf16[16,1024,128]{2,1,0:T(8,128)(2,1)} %stack.2), calls=%async_computation | async-start | bytes 8388608 | tf_op jit(solution)/shard_map/all_to_all | solution.py:54
  20.6 595.8 %reduce-scatter.2.cloned.1.call-start = ((), (), s32[]{:S(2)}) async-start(), calls=%async_computation.4 | async-start | bytes 4456448 | tf_op jit(solution)/shard_map/reduce_scatter | solution.py:154
  20.8 96.5 %copy-start.11 = (f32[16,64,2]{1,0,2:T(8,128)}, f32[16,64,2]{1,0,2:T(8,128)S(1)}, u32[]{:S(2)}) copy-start(f32[16,64,2]{1,0,2:T(8,128)S(1)} %reshape.213) | copy-start | bytes 24580
  25.2 92.1 %copy-start.35 = (f32[2048]{0:T(1024)S(1)}, f32[2048]{0:T(1024)}, u32[]{:S(2)}) copy-start(f32[2048]{0:T(1024)} %param.24) | copy-start | bytes 24580
  114.1 3.2 copy-start.32
  117.3 7.6 %copy-start.25 = (f32[1024]{0:T(1024)}, f32[1024]{0:T(1024)S(1)}, u32[]{:S(2)}) copy-start(f32[1024]{0:T(1024)S(1)} %add_rsqrt_fusion.3) | copy-start | bytes 12292
  117.3 3.8 copy-start.33
  121.1 3.8 copy-start.34
  129.4 5.4 collective-permute-start.1
  134.0 2.4 copy-start.17
  134.0 2.4 copy-start.18
  134.0 2.4 copy-start.19
  134.0 2.4 copy-start.20
  140.9 162.4 %copy-start.14 = (f32[2,16,64]{2,1,0:T(8,128)S(1)}, f32[2,16,64]{2,1,0:T(8,128)}, u32[]{:S(2)}) copy-start(f32[2,16,64]{2,1,0:T(8,128)} %get-tuple-element.187) | copy-start | bytes 24580
  308.0 3.3 copy-start.12
  311.3 1.7 copy-start.5
  311.3 1.9 copy-start.9
  313.1 2.1 copy-start.10
  315.2 10.6 %copy-start.3 = (f32[2,16,64,256]{3,2,1,0:T(8,128)}, f32[2,16,64,256]{3,2,1,0:T(8,128)S(1)}, u32[]{:S(2)}) copy-start(f32[2,16,64,256]{3,2,1,0:T(8,128)S(1)} %fusion.20) | copy-start | bytes 6291460
  315.2 5.2 copy-start.27
  397.4 5.1 collective-permute-start
  402.8 5.0 collective-permute-start
  408.1 5.0 collective-permute-start
  413.5 5.2 collective-permute-start
  418.9 6.9 collective-permute-start
  426.2 7.1 %collective-permute-start = (bf16[2,128,128]{2,1,0:T(8,128)(2,1)S(1)}, bf16[2,128,128]{2,1,0:T(8,128)(2,1)S(1)}, u32[]{:S(2)}, u32[]{:S(2)}) collective-permute-start(bf16[2,128,128]{2,1,0:T(8,128)(2,1)S(1)} %fusion.139), channel_id=1, source_target_pairs={{0,16},{16,32},{32,48},{48,64},{64,80},{80,96},{96,112},{112,128},... | collective-permute-start | bytes 196616 | tf_op jit(solution)/shard_map/while/body/eval_jaxpr/ppermute | solution.py:16
  433.6 7.7 %collective-permute-start = (bf16[2,128,128]{2,1,0:T(8,128)(2,1)S(1)}, bf16[2,128,128]{2,1,0:T(8,128)(2,1)S(1)}, u32[]{:S(2)}, u32[]{:S(2)}) collective-permute-start(bf16[2,128,128]{2,1,0:T(8,128)(2,1)S(1)} %fusion.139), channel_id=1, source_target_pairs={{0,16},{16,32},{32,48},{48,64},{64,80},{80,96},{96,112},{112,128},... | collective-permute-start | bytes 196616 | tf_op jit(solution)/shard_map/while/body/eval_jaxpr/ppermute | solution.py:16
  441.6 6.9 collective-permute-start
  448.8 7.1 %collective-permute-start = (bf16[2,128,128]{2,1,0:T(8,128)(2,1)S(1)}, bf16[2,128,128]{2,1,0:T(8,128)(2,1)S(1)}, u32[]{:S(2)}, u32[]{:S(2)}) collective-permute-start(bf16[2,128,128]{2,1,0:T(8,128)(2,1)S(1)} %fusion.139), channel_id=1, source_target_pairs={{0,16},{16,32},{32,48},{48,64},{64,80},{80,96},{96,112},{112,128},... | collective-permute-start | bytes 196616 | tf_op jit(solution)/shard_map/while/body/eval_jaxpr/ppermute | solution.py:16
  456.2 7.3 %collective-permute-start = (bf16[2,128,128]{2,1,0:T(8,128)(2,1)S(1)}, bf16[2,128,128]{2,1,0:T(8,128)(2,1)S(1)}, u32[]{:S(2)}, u32[]{:S(2)}) collective-permute-start(bf16[2,128,128]{2,1,0:T(8,128)(2,1)S(1)} %fusion.139), channel_id=1, source_target_pairs={{0,16},{16,32},{32,48},{48,64},{64,80},{80,96},{96,112},{112,128},... | collective-permute-start | bytes 196616 | tf_op jit(solution)/shard_map/while/body/eval_jaxpr/ppermute | solution.py:16
  463.8 7.1 %collective-permute-start = (bf16[2,128,128]{2,1,0:T(8,128)(2,1)S(1)}, bf16[2,128,128]{2,1,0:T(8,128)(2,1)S(1)}, u32[]{:S(2)}, u32[]{:S(2)}) collective-permute-start(bf16[2,128,128]{2,1,0:T(8,128)(2,1)S(1)} %fusion.139), channel_id=1, source_target_pairs={{0,16},{16,32},{32,48},{48,64},{64,80},{80,96},{96,112},{112,128},... | collective-permute-start | bytes 196616 | tf_op jit(solution)/shard_map/while/body/eval_jaxpr/ppermute | solution.py:16
  471.2 7.1 %collective-permute-start = (bf16[2,128,128]{2,1,0:T(8,128)(2,1)S(1)}, bf16[2,128,128]{2,1,0:T(8,128)(2,1)S(1)}, u32[]{:S(2)}, u32[]{:S(2)}) collective-permute-start(bf16[2,128,128]{2,1,0:T(8,128)(2,1)S(1)} %fusion.139), channel_id=1, source_target_pairs={{0,16},{16,32},{32,48},{48,64},{64,80},{80,96},{96,112},{112,128},... | collective-permute-start | bytes 196616 | tf_op jit(solution)/shard_map/while/body/eval_jaxpr/ppermute | solution.py:16
  478.6 7.1 %collective-permute-start = (bf16[2,128,128]{2,1,0:T(8,128)(2,1)S(1)}, bf16[2,128,128]{2,1,0:T(8,128)(2,1)S(1)}, u32[]{:S(2)}, u32[]{:S(2)}) collective-permute-start(bf16[2,128,128]{2,1,0:T(8,128)(2,1)S(1)} %fusion.139), channel_id=1, source_target_pairs={{0,16},{16,32},{32,48},{48,64},{64,80},{80,96},{96,112},{112,128},... | collective-permute-start | bytes 196616 | tf_op jit(solution)/shard_map/while/body/eval_jaxpr/ppermute | solution.py:16
  486.1 7.1 %collective-permute-start = (bf16[2,128,128]{2,1,0:T(8,128)(2,1)S(1)}, bf16[2,128,128]{2,1,0:T(8,128)(2,1)S(1)}, u32[]{:S(2)}, u32[]{:S(2)}) collective-permute-start(bf16[2,128,128]{2,1,0:T(8,128)(2,1)S(1)} %fusion.139), channel_id=1, source_target_pairs={{0,16},{16,32},{32,48},{48,64},{64,80},{80,96},{96,112},{112,128},... | collective-permute-start | bytes 196616 | tf_op jit(solution)/shard_map/while/body/eval_jaxpr/ppermute | solution.py:16
  493.5 7.4 %collective-permute-start = (bf16[2,128,128]{2,1,0:T(8,128)(2,1)S(1)}, bf16[2,128,128]{2,1,0:T(8,128)(2,1)S(1)}, u32[]{:S(2)}, u32[]{:S(2)}) collective-permute-start(bf16[2,128,128]{2,1,0:T(8,128)(2,1)S(1)} %fusion.139), channel_id=1, source_target_pairs={{0,16},{16,32},{32,48},{48,64},{64,80},{80,96},{96,112},{112,128},... | collective-permute-start | bytes 196616 | tf_op jit(solution)/shard_map/while/body/eval_jaxpr/ppermute | solution.py:16
  501.0 4.4 copy-start.4
  505.3 3.1 copy-start.1
  505.4 4.4 copy-start.15
  508.5 3.1 copy-start.13
  509.7 1.9 copy-start.2
  511.6 2.1 copy-start.6
  515.2 4.4 copy-start.26
  515.2 4.4 copy-start.36
  515.2 4.4 copy-start.38
  516.3 1.8 copy-start.8
  529.1 0.7 copy-start.23
  530.5 87.2 %copy-start.16 = (f32[2048]{0:T(1024)S(1)}, f32[2048]{0:T(1024)}, u32[]{:S(2)}) copy-start(f32[2048]{0:T(1024)} %param.36) | copy-start | bytes 24580
  619.3 37.0 %copy-start.31 = (bf16[1,2048,512]{2,1,0:T(8,128)(2,1)S(1)}, bf16[1,2048,512]{2,1,0:T(8,128)(2,1)}, u32[]{:S(2)}) copy-start(bf16[1,2048,512]{2,1,0:T(8,128)(2,1)} %param.39) | copy-start | bytes 6291460
  661.9 31.0 %copy-start.30 = (f32[64,2]{0,1:T(2,128)S(1)}, f32[64,2]{0,1:T(2,128)}, u32[]{:S(2)}) copy-start(f32[64,2]{0,1:T(2,128)} %param.38) | copy-start | bytes 1540
  661.9 31.4 %copy-start.7 = (bf16[64,2048]{1,0:T(8,128)(2,1)S(1)}, bf16[64,2048]{1,0:T(8,128)(2,1)}, u32[]{:S(2)}) copy-start(bf16[64,2048]{1,0:T(8,128)(2,1)} %reduce-scatter.2.cloned.1.call-done) | copy-start | bytes 786436
  661.9 31.0 %all-to-all-start.2 = ((bf16[1,16,16,2048]{3,2,0,1:T(8,128)(2,1)}), bf16[1,16,16,2048]{3,2,0,1:T(8,128)(2,1)S(1)}, u32[]{:S(2)}, u32[]{:S(2)}) async-start(bf16[1,16,16,2048]{3,2,0,1:T(8,128)(2,1)} %fusion.16), calls=%async_computation.3 | async-start | bytes 2097152 | tf_op jit(solution)/shard_map/all_to_all | solution.py:186
Sparse Core Ops, SparseCore 0:
  529.2 87.0 reduce-scatter.1
